TPU v7x, 256 devices: a whole 4x4x8 slice. The times are simulated.
256 devices in a mesh: seq: 32 (over z, x_hi, core), fsdp: 8 (over x_lo, y).
Axes of the slice: x: 4 (x_hi: 2, x_lo: 2; x = x_hi * 2 + x_lo), y: 4, z: 8, core: 2. Of those that a mesh axis runs over, the one named last changes fastest.
Arguments:
- text_states: bfloat16 [8192, 8192], P('seq'), may hold values from -6 to 6
- images: bfloat16 [32, 1601, 8192], P('seq', None, 'fsdp'), may hold values from -6 to 6
- norm_gain: float32 [8192], replicated, may hold values from 0.1 to 1.9
- query_weight: bfloat16 [8192, 4096], P('seq', 'fsdp'), may hold values from -0.0625 to 0.0625
- image_projection_weight: bfloat16 [8192, 2048], P(('fsdp', 'seq')), may hold values from -0.0625 to 0.0625
- query_gain: float32 [128], replicated, may hold values from 0.5 to 2
- key_gain: float32 [128], replicated, may hold values from 0.5 to 2
- admission: int32 [32, 32], P('seq'), may hold values from 0 to 1, as said below
Outputs:
- attended: bfloat16 [8192, 4096], P('seq', 'fsdp')
Inputs may be any that keep to these rules, and one draw needn't show every extreme that they name: admission[c, m] is 1 for m = c and for at most 2 of the images m with c - 4 <= m < c, and 0 elsewhere; in every draw some text blocks, the last one among them, attend to exactly 3 images.
All inputs are finite; a program needn't handle non-finite values.
Results may differ from a plain program's by a relative error of at most 0.035.
Values may be sent and summed in bfloat16 or wider, within the bound.
No kernel may reach another device: no remote copies, remote signals or barrier semaphores. Data moves between devices by JAX's collectives and lax.ppermute only.
A program may use at most 128 MiB of HBM per device.

v0:
```python
import math
import jax
import jax.numpy as jnp
from jax import lax
from jax.sharding import PartitionSpec as P

KEY_VALUE_HEADS = 8
IMAGE_LOOKBACK = 4


def from_behind(value, axis, steps):
    count = lax.axis_size(axis)
    initial, last = (max(0, -steps), min(count, count - steps))
    return lax.ppermute(value, axis, [(source, source + steps) for source in range(initial, last)])


def rms_scale(values, gain):
    return values * lax.rsqrt(jnp.mean(values * values, axis=-1, keepdims=True) + 1e-05) * gain


def attend(query_heads, stacked, admitted):
    slot_count, kv_heads, image_tokens, double_width = stacked.shape
    head_dim = double_width // 2
    row_count, heads_local, _ = query_heads.shape
    heads_per_group = heads_local // kv_heads
    grouped = query_heads.reshape(row_count, kv_heads, heads_per_group, head_dim)
    grouped = grouped.transpose(1, 2, 0, 3).reshape(kv_heads, heads_per_group * row_count, head_dim)
    per_head = jnp.moveaxis(stacked, 1, 0).reshape(
        kv_heads, slot_count * image_tokens, double_width
    )
    column_live = jnp.repeat(admitted, image_tokens)
    score_scale = 1.0 / math.sqrt(head_dim)

    def one_head(operands):
        query_rows, key_value_pair = operands
        scores = (
            lax.dot_general(
                query_rows,
                key_value_pair[:, :head_dim],
                (((1,), (1,)), ((), ())),
                preferred_element_type=jnp.float32,
            )
            * score_scale
        )
        scores = jnp.where(column_live[None, :], scores, -jnp.inf)
        row_peak = jnp.max(scores, axis=1, keepdims=True)
        weights = jnp.exp(scores - row_peak)
        row_total = jnp.sum(weights, axis=1, keepdims=True)
        blended = jnp.dot(
            weights.astype(jnp.bfloat16),
            key_value_pair[:, head_dim:],
            preferred_element_type=jnp.float32,
        )
        return blended / row_total

    outputs = lax.map(one_head, (grouped, per_head))
    outputs = outputs.reshape(kv_heads, heads_per_group, row_count, head_dim).transpose(2, 0, 1, 3)
    return outputs.reshape(row_count, heads_local * head_dim).astype(jnp.bfloat16)


def on_device(
    text_states,
    images,
    norm_gain,
    query_weight,
    image_projection_weight,
    query_gain,
    key_gain,
    admission,
):
    head_dim = query_gain.shape[0]
    local_key_value = KEY_VALUE_HEADS // lax.axis_size("fsdp")
    heads_local = query_weight.shape[1] // head_dim
    row_count = text_states.shape[0]
    normed = rms_scale(text_states.astype(jnp.float32), norm_gain).astype(jnp.bfloat16)
    columns = normed
    queries = jnp.dot(
        columns,
        lax.all_gather(query_weight, "seq", axis=0, tiled=True),
        preferred_element_type=jnp.float32,
    )
    query_heads = rms_scale(queries.reshape(row_count, heads_local, head_dim), query_gain).astype(
        jnp.bfloat16
    )
    weight_block = lax.all_gather(image_projection_weight, "seq", axis=0, tiled=True)
    features = images[0]
    columns = weight_block
    score_product = jnp.dot(features, columns, preferred_element_type=jnp.float32)
    own_kv = lax.psum_scatter(
        score_product.reshape(
            features.shape[0], local_key_value * lax.axis_size("fsdp"), 2 * head_dim
        )
        .transpose(1, 0, 2)
        .astype(jnp.bfloat16),
        "fsdp",
        scatter_dimension=0,
        tiled=True,
    ).astype(jnp.float32)
    key_part = rms_scale(own_kv[..., :head_dim], key_gain)
    packed = jnp.concatenate([key_part, own_kv[..., head_dim:]], axis=-1).astype(jnp.bfloat16)
    image_window = [packed]
    for distance in range(1, IMAGE_LOOKBACK + 1):
        image_window.append(from_behind(packed, "seq", distance))
    stacked = jnp.stack(image_window)
    span_index = lax.axis_index("seq")
    image_ids = span_index - jnp.arange(IMAGE_LOOKBACK + 1, dtype=jnp.int32)
    admitted = (image_ids >= 0) & (jnp.take(admission[0], jnp.maximum(image_ids, 0)) == 1)
    return attend(query_heads, stacked, admitted)


def solution(mesh):
    placed = (
        P("seq", None),
        P("seq", None, "fsdp"),
        P(),
        P("seq", "fsdp"),
        P(("fsdp", "seq"), None),
        P(),
        P(),
        P("seq", None),
    )
    return jax.shard_map(
        on_device, mesh=mesh, in_specs=placed, out_specs=P("seq", "fsdp"), check_vma=False
    )
```

profile of v0, /device:TPU:129, one launch (start us, length us, event | category | flops | bytes accessed | tf_op | source)
XLA Modules:
  0.0 410.5 jit_solution(13469132266472897213)
XLA Ops:
  8.1 88.1 %all-gather.5.cloned.1.call-done = bf16[1024,2048]{1,0:T(8,128)(2,1)} async-done(((bf16[32,2048]{1,0:T(8,128)(2,1)}), bf16[1024,2048]{1,0:T(8,128)(2,1)}) %all-gather.5.cloned.1.call-update) | async-done | bytes 4194320 | tf_op jit(solution)/shard_map/all_gather | solution.py:85
  96.1 6.4 %copy.20 = bf16[2048,1024]{1,0:T(8,128)(2,1)} copy(bf16[2048,1024]{0,1:T(8,128)(2,1)} %bitcast.39) | data formatting | bytes 8388608 | tf_op jit(solution)/shard_map/dot_general | solution.py:88
  102.5 11.0 %convert_bitcast_fusion = bf16[8,1601,256]{2,1,0:T(8,128)(2,1)} fusion(bf16[8,256,1024]{2,1,0:T(8,128)(2,1)} %bitcast.40, bf16[1,1601,1024]{2,1,0:T(8,128)(2,1)S(1)} %copy-done), kind=kOutput, calls=%fused_computation.13 | convolution fusion | flops 6718359552 | bytes 14030848 | tf_op jit(solution)/shard_map/dot_general | solution.py:88
  115.0 3.1 fusion.6
  118.1 78.7 %all-gather.3.cloned.1.call-done = bf16[8192,512]{1,0:T(8,128)(2,1)} async-done(((bf16[256,512]{1,0:T(8,128)(2,1)}), bf16[8192,512]{1,0:T(8,128)(2,1)}) %all-gather.3.cloned.1.call-update) | async-done | bytes 8388624 | tf_op jit(solution)/shard_map/all_gather | solution.py:79
  196.8 7.0 %fusion.31 = (f32[256,512]{1,0:T(8,128)S(1)}, f32[256,512]{1,0:T(8,128)S(1)}) fusion(bf16[8192,512]{1,0:T(8,128)(2,1)} %all-gather.3.cloned.1.call-done, bf16[256,8192]{1,0:T(8,128)(2,1)} %param.8, f32[8192]{0:T(1024)S(1)} %copy-done.7, f32[256]{0:T(256)S(1)} %add_rsqrt_fusion.2), kind=kOutput, calls=%fused_computation.45 | convolution fusion | flops 2156003328 | bytes 13665280 | tf_op jit(solution)/shard_map/dot_general | solution.py:77
  204.9 72.2 %reduce-scatter.2.cloned.1.call-done = bf16[1,1601,256]{2,1,0:T(8,128)(2,1)} async-done(((bf16[8,1601,256]{2,1,0:T(8,128)(2,1)}), bf16[1,1601,256]{2,1,0:T(8,128)(2,1)}) %reduce-scatter.2.cloned.1.call-update) | async-done | bytes 819728 | tf_op jit(solution)/shard_map/reduce_scatter | solution.py:89
  277.1 1.4 convert_element_type.62
  279.3 4.8 %collective-permute-start = (bf16[1,1601,256]{2,1,0:T(8,128)(2,1)S(1)}, bf16[1,1601,256]{2,1,0:T(8,128)(2,1)S(1)}, u32[]{:S(2)}, u32[]{:S(2)}) collective-permute-start(bf16[1,1601,256]{2,1,0:T(8,128)(2,1)S(1)} %pad_maximum_fusion), channel_id=1, source_target_pairs={{0,8},{8,16},{16,24},{24,32},{32,40},{40,48},{48,56},{56,64},{64,7... | collective-permute-start | bytes 2459144 | tf_op jit(solution)/shard_map/ppermute | solution.py:14
  284.4 2.3 collective-permute-start.3
  286.7 1.9 collective-permute-start.2
  288.6 2.7 collective-permute-start.1
  291.4 1.0 maximum_dynamic-update-slice_fusion
  292.4 4.1 collective-permute-done
  296.5 1.0 bitcast_dynamic-update-slice_fusion.3
  297.4 52.0 %collective-permute-done.1 = bf16[1,1601,256]{2,1,0:T(8,128)(2,1)S(1)} collective-permute-done((bf16[1,1601,256]{2,1,0:T(8,128)(2,1)S(1)}, bf16[1,1601,256]{2,1,0:T(8,128)(2,1)S(1)}, u32[]{:S(2)}, u32[]{:S(2)}) %collective-permute-start.1) | collective-permute-done | bytes 819744 | tf_op jit(solution)/shard_map/ppermute | solution.py:14
  349.5 1.0 bitcast_dynamic-update-slice_fusion.2
  350.4 1.0 bitcast_dynamic-update-slice_fusion.1
  351.4 1.0 bitcast_dynamic-update-slice_fusion
  352.3 5.2 %squeeze.19 = bf16[8005,256]{1,0:T(8,128)(2,1)} reshape(bf16[5,1,1601,256]{3,2,1,0:T(8,128)(2,1)} %bitcast_dynamic-update-slice_fusion) | data formatting | bytes 8197120 | tf_op jit(solution)/shard_map/while/body/jit(dynamic_index_in_dim)/squeeze | solution.py:56
  357.5 13.8 %fusion = (f32[1024]{0:T(1024)S(1)}, f32[1024,8005]{0,1:T(8,128)}) fusion(pred[8005]{0:T(1024)(128)(4,1)S(1)} %broadcast_in_dim.38, bf16[1024,128]{1,0:T(8,128)(2,1)S(1)} %bitcast.41, bf16[8005,256]{1,0:T(8,128)(2,1)} %squeeze.19), kind=kOutput, calls=%fused_computation.3 | convolution fusion | flops 2123053056 | bytes 35112772 | tf_op jit(solution)/shard_map/while/body/eval_jaxpr/dot_general | solution.py:37
  371.4 15.1 %fusion.1 = f32[1024]{0:T(1024)S(1)} fusion(f32[1024,8005]{0,1:T(8,128)} %get-tuple-element.22, f32[1024]{0:T(1024)S(1)} %get-tuple-element.20, pred[8005]{0:T(1024)(128)(4,1)S(1)} %broadcast_in_dim.38), kind=kLoop, calls=%fused_computation.4 | loop fusion | flops 32787456 | bytes 32804676 | tf_op jit(solution)/shard_map/while/body/eval_jaxpr/reduce_sum | solution.py:48
  386.5 16.6 %fusion.22 = bf16[1024,128]{1,0:T(8,128)(2,1)S(1)} fusion(bf16[8005,256]{1,0:T(8,128)(2,1)S(1)} %copy-done.3, f32[1024,8005]{0,1:T(8,128)} %get-tuple-element.22, f32[1024]{0:T(1024)S(1)} %get-tuple-element.20, pred[8005]{0:T(1024)(128)(4,1)S(1)} %broadcast_in_dim.38, f32[1024]{0:T(1024)S(1)} %fusion.1), kind=kOutput, calls=%fused_computation.22 | convolution fusion | flops 2131513344 | bytes 35117056 | tf_op jit(solution)/shard_map/while/body/eval_jaxpr/dot_general | solution.py:49
  403.3 0.7 copy.29
  (46 shorter events, 5.2 us)
Async XLA Ops:
  6.5 96.0 %copy-start = (bf16[1,1601,1024]{2,1,0:T(8,128)(2,1)S(1)}, bf16[1,1601,1024]{2,1,0:T(8,128)(2,1)}, u32[]{:S(2)}) copy-start(bf16[1,1601,1024]{2,1,0:T(8,128)(2,1)} %param.9) | copy-start | bytes 9836548
  6.5 89.6 %all-gather.5.cloned.1.call-start = ((), (), s32[]{:S(2)}) async-start(), calls=%async_computation.2 | async-start | bytes 4325376 | tf_op jit(solution)/shard_map/all_gather | solution.py:85
  7.3 189.5 %all-gather.3.cloned.1.call-start = ((), (), s32[]{:S(2)}) async-start(), calls=%async_computation.1 | async-start | bytes 8650752 | tf_op jit(solution)/shard_map/all_gather | solution.py:79
  8.0 269.1 %reduce-scatter.2.cloned.1.call-start = ((), (), s32[]{:S(2)}) async-start(), calls=%async_computation.3 | async-start | bytes 7409664 | tf_op jit(solution)/shard_map/reduce_scatter | solution.py:89
  113.5 0.7 copy-start.2
  113.5 83.3 %copy-start.7 = (f32[8192]{0:T(1024)S(1)}, f32[8192]{0:T(1024)}, u32[]{:S(2)}) copy-start(f32[8192]{0:T(1024)} %param.10) | copy-start | bytes 98308
  118.1 86.6 %copy-start.6 = (f32[128]{0:T(128)S(1)}, f32[128]{0:T(128)}, u32[]{:S(2)}) copy-start(f32[128]{0:T(128)} %param.13) | copy-start | bytes 1540
  203.9 75.0 %copy-start.5 = (f32[128]{0:T(128)S(1)}, f32[128]{0:T(128)}, u32[]{:S(2)}) copy-start(f32[128]{0:T(128)} %param.14) | copy-start | bytes 1540
  277.1 2.0 slice-start
  277.1 14.2 %copy-start.4 = (bf16[1,1601,256]{2,1,0:T(8,128)(2,1)S(1)}, bf16[1,1601,256]{2,1,0:T(8,128)(2,1)}, u32[]{:S(2)}) copy-start(bf16[1,1601,256]{2,1,0:T(8,128)(2,1)} %reduce-scatter.2.cloned.1.call-done) | copy-start | bytes 2459140
  279.3 17.2 %collective-permute-start = (bf16[1,1601,256]{2,1,0:T(8,128)(2,1)S(1)}, bf16[1,1601,256]{2,1,0:T(8,128)(2,1)S(1)}, u32[]{:S(2)}, u32[]{:S(2)}) collective-permute-start(bf16[1,1601,256]{2,1,0:T(8,128)(2,1)S(1)} %pad_maximum_fusion), channel_id=1, source_target_pairs={{0,8},{8,16},{16,24},{24,32},{32,40},{40,48},{48,56},{56,64},{64,7... | collective-permute-start | bytes 2459144 | tf_op jit(solution)/shard_map/ppermute | solution.py:14
  284.4 67.0 %collective-permute-start.3 = (bf16[1,1601,256]{2,1,0:T(8,128)(2,1)S(1)}, bf16[1,1601,256]{2,1,0:T(8,128)(2,1)S(1)}, u32[]{:S(2)}, u32[]{:S(2)}) collective-permute-start(bf16[1,1601,256]{2,1,0:T(8,128)(2,1)S(1)} %pad_maximum_fusion), channel_id=1, source_target_pairs={{0,32},{8,40},{16,48},{24,56},{32,64},{40,72},{48,80},{56,88},{64,... | collective-permute-start | bytes 2459144 | tf_op jit(solution)/shard_map/ppermute | solution.py:14
  286.7 63.7 %collective-permute-start.2 = (bf16[1,1601,256]{2,1,0:T(8,128)(2,1)S(1)}, bf16[1,1601,256]{2,1,0:T(8,128)(2,1)S(1)}, u32[]{:S(2)}, u32[]{:S(2)}) collective-permute-start(bf16[1,1601,256]{2,1,0:T(8,128)(2,1)S(1)} %pad_maximum_fusion), channel_id=1, source_target_pairs={{0,24},{8,32},{16,40},{24,48},{32,56},{40,64},{48,72},{56,80},{64,... | collective-permute-start | bytes 2459144 | tf_op jit(solution)/shard_map/ppermute | solution.py:14
  288.6 60.8 %collective-permute-start.1 = (bf16[1,1601,256]{2,1,0:T(8,128)(2,1)S(1)}, bf16[1,1601,256]{2,1,0:T(8,128)(2,1)S(1)}, u32[]{:S(2)}, u32[]{:S(2)}) collective-permute-start(bf16[1,1601,256]{2,1,0:T(8,128)(2,1)S(1)} %pad_maximum_fusion), channel_id=1, source_target_pairs={{0,16},{8,24},{16,32},{24,40},{32,48},{40,56},{48,64},{56,72},{64,... | collective-permute-start | bytes 2459144 | tf_op jit(solution)/shard_map/ppermute | solution.py:14
  371.4 15.1 %copy-start.3 = (bf16[8005,256]{1,0:T(8,128)(2,1)S(1)}, bf16[8005,256]{1,0:T(8,128)(2,1)}, u32[]{:S(2)}) copy-start(bf16[8005,256]{1,0:T(8,128)(2,1)} %squeeze.19) | copy-start | bytes 12295684
  386.4 17.6 %copy-start.1 = (bf16[1,1601,1024]{2,1,0:T(8,128)(2,1)S(1)}, bf16[1,1601,1024]{2,1,0:T(8,128)(2,1)}, u32[]{:S(2)}) copy-start(bf16[1,1601,1024]{2,1,0:T(8,128)(2,1)} %param.9) | copy-start | bytes 9836548
Sparse Core Ops, SparseCore 0:
  10.1 85.9 all-gather.4
  98.9 97.8 all-gather.2
  199.4 77.6 reduce-scatter.1
where the time goes:
time: 411 us
  waiting for transfers between devices  296 us (72%)
  matrix products  48.4 us (12%)
  other arithmetic  22.1 us (5%)
  local copies, waits for them, and re-layouts  18.3 us (4%)
  between operations  13.4 us (3%)
  starting transfers between devices  11.9 us (3%)
    all_gather x1, waiting for transfers between devices, on_device(): lax.all_gather(image_projection_weight, 'seq', axis=0, tiled=True)  88.1 us
    all_gather x1, waiting for transfers between devices, on_device(): lax.all_gather(query_weight, 'seq', axis=0, tiled=True)  78.7 us
    reduce_scatter x1, waiting for transfers between devices, on_device(): lax.psum_scatter(score_product.reshape(features.shape[0], local_key_value...  72.2 us
    ppermute x4, waiting for transfers between devices, from_behind(): lax.ppermute(value, axis, [(source, source + steps) for source in range(i...  56.1 us
    dot_general x1, matrix products, one_head(): jnp.dot(weights.astype(jnp.bfloat16), key_value_pair[:, head_dim:], prefe...  16.6 us
    reduce_sum x1, other arithmetic, one_head(): row_total = jnp.sum(weights, axis=1, keepdims=True)  15.1 us
    dot_general x1, matrix products, one_head(): lax.dot_general(query_rows, key_value_pair[:, :head_dim], (((1,), (1,)),...  13.8 us
    ppermute x4, starting transfers between devices, from_behind(): lax.ppermute(value, axis, [(source, source + steps) for source in range(i...  11.8 us
  transfers between devices with their start and end apart: 7, of which 5 were waited for; matrix products, arithmetic and copies ran while one was open for 8% of the time, Pallas kernels for 0%

commit v1 on v0

--- a/solution.py
+++ b/solution.py
@@ -82,7 +82,10 @@
     query_heads = rms_scale(queries.reshape(row_count, heads_local, head_dim), query_gain).astype(
         jnp.bfloat16
     )
-    weight_block = lax.all_gather(image_projection_weight, "seq", axis=0, tiled=True)
+    weight_block = jnp.concatenate(
+        lax.all_to_all(jnp.stack([image_projection_weight] * lax.axis_size("seq")), "seq", 0, 0),
+        axis=0,
+    )
     features = images[0]
     columns = weight_block
     score_product = jnp.dot(features, columns, preferred_element_type=jnp.float32)

time: 411 us -> 365 us (0.89)
  waiting for transfers between devices: 296 us -> 123 us
  blocking collectives: 0 us -> 123 us
    all_to_all x0 -> x1, blocking collectives: none -> 123 us  [on_device(): lax.all_to_all(jnp.stack([image_projection_weight] * lax.axis_size('seq')...]
    all_gather x1 -> x0, waiting for transfers between devices: 88.1 us -> none  [on_device(): lax.all_gather(image_projection_weight, 'seq', axis=0, tiled=True)]
    all_gather x1, waiting for transfers between devices: 78.7 us -> 0.02 us  [on_device(): lax.all_gather(query_weight, 'seq', axis=0, tiled=True)]
    reduce_scatter x1, waiting for transfers between devices: 72.2 us -> 66.5 us  [on_device(): lax.psum_scatter(score_product.reshape(features.shape[0], local_key_value...]
  transfers between devices with their start and end apart: 7 -> 6, of which waited for: 5 -> 3; matrix products, arithmetic and copies ran while one was open for 8% -> 10% of each run, Pallas kernels for 0% -> 0%
where the time goes in v1:
time: 365 us; the launch traced here: 364 us
  waiting for transfers between devices  123 us (34%)
  blocking collectives  123 us (34%)
  matrix products  48.6 us (13%)
  other arithmetic  22.1 us (6%)
  local copies, waits for them, and re-layouts  19.9 us (5%)
  between operations  15.1 us (4%)
  starting transfers between devices  11.9 us (3%)
    all_to_all x1, blocking collectives, on_device(): lax.all_to_all(jnp.stack([image_projection_weight] * lax.axis_size('seq')...  123 us
    reduce_scatter x1, waiting for transfers between devices, on_device(): lax.psum_scatter(score_product.reshape(features.shape[0], local_key_value...  66.5 us
    ppermute x4, waiting for transfers between devices, from_behind(): lax.ppermute(value, axis, [(source, source + steps) for source in range(i...  56.1 us
    dot_general x1, matrix products, one_head(): jnp.dot(weights.astype(jnp.bfloat16), key_value_pair[:, head_dim:], prefe...  16.6 us
    reduce_sum x1, other arithmetic, one_head(): row_total = jnp.sum(weights, axis=1, keepdims=True)  15.1 us
    dot_general x1, matrix products, one_head(): lax.dot_general(query_rows, key_value_pair[:, :head_dim], (((1,), (1,)),...  13.8 us
    ppermute x4, starting transfers between devices, from_behind(): lax.ppermute(value, axis, [(source, source + steps) for source in range(i...  11.9 us
    dot_general x1, matrix products, on_device(): jnp.dot(features, columns, preferred_element_type=jnp.float32)  11.2 us
  transfers between devices with their start and end apart: 6, of which 3 were waited for; matrix products, arithmetic and copies ran while one was open for 10% of the time, Pallas kernels for 0%

profile of v1, /device:TPU:129, one launch (start us, length us, event | category | flops | bytes accessed | tf_op | source)
XLA Modules:
  0.0 363.8 jit_solution(11948679769578988679)
XLA Ops:
  8.1 1.6 stack.12
  9.8 122.8 %all_to_all.5 = bf16[32,32,2048]{2,1,0:T(8,128)(2,1)} all-to-all(bf16[32,32,2048]{2,1,0:T(8,128)(2,1)S(1)} %stack.12), channel_id=1, replica_groups=mesh['seq'=32,'fsdp'=8] {'seq'}, dimensions={0} | all-to-all | bytes 8388608 | tf_op jit(solution)/shard_map/all_to_all | solution.py:86
  132.6 6.4 %copy.20 = bf16[2048,1024]{1,0:T(8,128)(2,1)} copy(bf16[2048,1024]{0,1:T(8,128)(2,1)} %bitcast.41) | data formatting | bytes 8388608 | tf_op jit(solution)/shard_map/dot_general | solution.py:91
  139.0 11.2 %convert_bitcast_fusion = bf16[8,1601,256]{2,1,0:T(8,128)(2,1)} fusion(bf16[8,256,1024]{2,1,0:T(8,128)(2,1)} %bitcast.42, bf16[1,1601,1024]{2,1,0:T(8,128)(2,1)S(1)} %copy-done), kind=kOutput, calls=%fused_computation.13 | convolution fusion | flops 6718359552 | bytes 14030848 | tf_op jit(solution)/shard_map/dot_general | solution.py:91
  151.7 3.1 fusion.6
  154.9 7.0 %fusion.31 = (f32[256,512]{1,0:T(8,128)S(1)}, f32[256,512]{1,0:T(8,128)S(1)}) fusion(bf16[8192,512]{1,0:T(8,128)(2,1)} %all-gather.2.cloned.1.call-done, bf16[256,8192]{1,0:T(8,128)(2,1)} %param.8, f32[8192]{0:T(1024)S(1)} %copy-done.7, f32[256]{0:T(256)S(1)} %add_rsqrt_fusion.2), kind=kOutput, calls=%fused_computation.45 | convolution fusion | flops 2156003328 | bytes 13665280 | tf_op jit(solution)/shard_map/dot_general | solution.py:77
  163.0 66.5 %reduce-scatter.2.cloned.1.call-done = bf16[1,1601,256]{2,1,0:T(8,128)(2,1)} async-done(((bf16[8,1601,256]{2,1,0:T(8,128)(2,1)}), bf16[1,1601,256]{2,1,0:T(8,128)(2,1)}) %reduce-scatter.2.cloned.1.call-update) | async-done | bytes 819728 | tf_op jit(solution)/shard_map/reduce_scatter | solution.py:92
  229.4 1.4 convert_element_type.62
  231.6 4.9 %collective-permute-start = (bf16[1,1601,256]{2,1,0:T(8,128)(2,1)S(1)}, bf16[1,1601,256]{2,1,0:T(8,128)(2,1)S(1)}, u32[]{:S(2)}, u32[]{:S(2)}) collective-permute-start(bf16[1,1601,256]{2,1,0:T(8,128)(2,1)S(1)} %pad_maximum_fusion), channel_id=1, source_target_pairs={{0,8},{8,16},{16,24},{24,32},{32,40},{40,48},{48,56},{56,64},{64,7... | collective-permute-start | bytes 2459144 | tf_op jit(solution)/shard_map/ppermute | solution.py:14
  236.8 2.3 collective-permute-start.3
  239.1 1.9 collective-permute-start.2
  241.0 2.8 collective-permute-start.1
  243.8 1.0 maximum_dynamic-update-slice_fusion
  244.8 4.0 %collective-permute-done = bf16[1,1601,256]{2,1,0:T(8,128)(2,1)S(1)} collective-permute-done((bf16[1,1601,256]{2,1,0:T(8,128)(2,1)S(1)}, bf16[1,1601,256]{2,1,0:T(8,128)(2,1)S(1)}, u32[]{:S(2)}, u32[]{:S(2)}) %collective-permute-start) | collective-permute-done | bytes 819744 | tf_op jit(solution)/shard_map/ppermute | solution.py:14
  248.8 1.0 bitcast_dynamic-update-slice_fusion.3
  249.8 52.0 %collective-permute-done.1 = bf16[1,1601,256]{2,1,0:T(8,128)(2,1)S(1)} collective-permute-done((bf16[1,1601,256]{2,1,0:T(8,128)(2,1)S(1)}, bf16[1,1601,256]{2,1,0:T(8,128)(2,1)S(1)}, u32[]{:S(2)}, u32[]{:S(2)}) %collective-permute-start.1) | collective-permute-done | bytes 819744 | tf_op jit(solution)/shard_map/ppermute | solution.py:14
  301.8 0.9 bitcast_dynamic-update-slice_fusion.2
  302.8 0.9 bitcast_dynamic-update-slice_fusion.1
  303.7 1.0 bitcast_dynamic-update-slice_fusion
  304.7 5.2 %squeeze.19 = bf16[8005,256]{1,0:T(8,128)(2,1)} reshape(bf16[5,1,1601,256]{3,2,1,0:T(8,128)(2,1)} %bitcast_dynamic-update-slice_fusion) | data formatting | bytes 8197120 | tf_op jit(solution)/shard_map/while/body/jit(dynamic_index_in_dim)/squeeze | solution.py:56
  309.9 13.8 %fusion = (f32[1024]{0:T(1024)S(1)}, f32[1024,8005]{0,1:T(8,128)}) fusion(pred[8005]{0:T(1024)(128)(4,1)S(1)} %broadcast_in_dim.38, bf16[1024,128]{1,0:T(8,128)(2,1)S(1)} %bitcast.43, bf16[8005,256]{1,0:T(8,128)(2,1)} %squeeze.19), kind=kOutput, calls=%fused_computation.3 | convolution fusion | flops 2123053056 | bytes 35112772 | tf_op jit(solution)/shard_map/while/body/eval_jaxpr/dot_general | solution.py:37
  323.7 15.1 %fusion.1 = f32[1024]{0:T(1024)S(1)} fusion(f32[1024,8005]{0,1:T(8,128)} %get-tuple-element.22, f32[1024]{0:T(1024)S(1)} %get-tuple-element.20, pred[8005]{0:T(1024)(128)(4,1)S(1)} %broadcast_in_dim.38), kind=kLoop, calls=%fused_computation.4 | loop fusion | flops 32787456 | bytes 32804676 | tf_op jit(solution)/shard_map/while/body/eval_jaxpr/reduce_sum | solution.py:48
  338.8 16.6 %fusion.22 = bf16[1024,128]{1,0:T(8,128)(2,1)S(1)} fusion(bf16[8005,256]{1,0:T(8,128)(2,1)S(1)} %copy-done.3, f32[1024,8005]{0,1:T(8,128)} %get-tuple-element.22, f32[1024]{0:T(1024)S(1)} %get-tuple-element.20, pred[8005]{0:T(1024)(128)(4,1)S(1)} %broadcast_in_dim.38, f32[1024]{0:T(1024)S(1)} %fusion.1), kind=kOutput, calls=%fused_computation.22 | convolution fusion | flops 2131513344 | bytes 35117056 | tf_op jit(solution)/shard_map/while/body/eval_jaxpr/dot_general | solution.py:49
  355.6 0.7 copy.29
  (45 shorter events, 4.5 us)
Async XLA Ops:
  7.4 131.7 %copy-start = (bf16[1,1601,1024]{2,1,0:T(8,128)(2,1)S(1)}, bf16[1,1601,1024]{2,1,0:T(8,128)(2,1)}, u32[]{:S(2)}) copy-start(bf16[1,1601,1024]{2,1,0:T(8,128)(2,1)} %param.9) | copy-start | bytes 9836548
  7.4 147.5 %all-gather.2.cloned.1.call-start = ((), (), s32[]{:S(2)}) async-start(), calls=%async_computation.2 | async-start | bytes 8650752 | tf_op jit(solution)/shard_map/all_gather | solution.py:79
  8.1 221.3 %reduce-scatter.2.cloned.1.call-start = ((), (), s32[]{:S(2)}) async-start(), calls=%async_computation.3 | async-start | bytes 7409664 | tf_op jit(solution)/shard_map/reduce_scatter | solution.py:92
  150.2 0.7 copy-start.2
  150.2 4.7 %copy-start.7 = (f32[8192]{0:T(1024)S(1)}, f32[8192]{0:T(1024)}, u32[]{:S(2)}) copy-start(f32[8192]{0:T(1024)} %param.10) | copy-start | bytes 98308
  154.8 7.9 %copy-start.6 = (f32[128]{0:T(128)S(1)}, f32[128]{0:T(128)}, u32[]{:S(2)}) copy-start(f32[128]{0:T(128)} %param.13) | copy-start | bytes 1540
  161.9 69.3 %copy-start.5 = (f32[128]{0:T(128)S(1)}, f32[128]{0:T(128)}, u32[]{:S(2)}) copy-start(f32[128]{0:T(128)} %param.14) | copy-start | bytes 1540
  229.4 2.0 slice-start
  229.4 14.3 %copy-start.4 = (bf16[1,1601,256]{2,1,0:T(8,128)(2,1)S(1)}, bf16[1,1601,256]{2,1,0:T(8,128)(2,1)}, u32[]{:S(2)}) copy-start(bf16[1,1601,256]{2,1,0:T(8,128)(2,1)} %reduce-scatter.2.cloned.1.call-done) | copy-start | bytes 2459140
  231.6 17.3 %collective-permute-start = (bf16[1,1601,256]{2,1,0:T(8,128)(2,1)S(1)}, bf16[1,1601,256]{2,1,0:T(8,128)(2,1)S(1)}, u32[]{:S(2)}, u32[]{:S(2)}) collective-permute-start(bf16[1,1601,256]{2,1,0:T(8,128)(2,1)S(1)} %pad_maximum_fusion), channel_id=1, source_target_pairs={{0,8},{8,16},{16,24},{24,32},{32,40},{40,48},{48,56},{56,64},{64,7... | collective-permute-start | bytes 2459144 | tf_op jit(solution)/shard_map/ppermute | solution.py:14
  236.8 67.0 %collective-permute-start.3 = (bf16[1,1601,256]{2,1,0:T(8,128)(2,1)S(1)}, bf16[1,1601,256]{2,1,0:T(8,128)(2,1)S(1)}, u32[]{:S(2)}, u32[]{:S(2)}) collective-permute-start(bf16[1,1601,256]{2,1,0:T(8,128)(2,1)S(1)} %pad_maximum_fusion), channel_id=1, source_target_pairs={{0,32},{8,40},{16,48},{24,56},{32,64},{40,72},{48,80},{56,88},{64,... | collective-permute-start | bytes 2459144 | tf_op jit(solution)/shard_map/ppermute | solution.py:14
  239.1 63.7 %collective-permute-start.2 = (bf16[1,1601,256]{2,1,0:T(8,128)(2,1)S(1)}, bf16[1,1601,256]{2,1,0:T(8,128)(2,1)S(1)}, u32[]{:S(2)}, u32[]{:S(2)}) collective-permute-start(bf16[1,1601,256]{2,1,0:T(8,128)(2,1)S(1)} %pad_maximum_fusion), channel_id=1, source_target_pairs={{0,24},{8,32},{16,40},{24,48},{32,56},{40,64},{48,72},{56,80},{64,... | collective-permute-start | bytes 2459144 | tf_op jit(solution)/shard_map/ppermute | solution.py:14
  241.0 60.9 %collective-permute-start.1 = (bf16[1,1601,256]{2,1,0:T(8,128)(2,1)S(1)}, bf16[1,1601,256]{2,1,0:T(8,128)(2,1)S(1)}, u32[]{:S(2)}, u32[]{:S(2)}) collective-permute-start(bf16[1,1601,256]{2,1,0:T(8,128)(2,1)S(1)} %pad_maximum_fusion), channel_id=1, source_target_pairs={{0,16},{8,24},{16,32},{24,40},{32,48},{40,56},{48,64},{56,72},{64,... | collective-permute-start | bytes 2459144 | tf_op jit(solution)/shard_map/ppermute | solution.py:14
  323.7 15.1 %copy-start.3 = (bf16[8005,256]{1,0:T(8,128)(2,1)S(1)}, bf16[8005,256]{1,0:T(8,128)(2,1)}, u32[]{:S(2)}) copy-start(bf16[8005,256]{1,0:T(8,128)(2,1)} %squeeze.19) | copy-start | bytes 12295684
  338.8 17.6 %copy-start.1 = (bf16[1,1601,1024]{2,1,0:T(8,128)(2,1)S(1)}, bf16[1,1601,1024]{2,1,0:T(8,128)(2,1)}, u32[]{:S(2)}) copy-start(bf16[1,1601,1024]{2,1,0:T(8,128)(2,1)} %param.9) | copy-start | bytes 9836548
Sparse Core Ops, SparseCore 0:
  11.4 135.1 all-gather.1
Sparse Core Ops, SparseCore 1:
  150.3 79.0 reduce-scatter.1
